TPU v7x, 256 devices: a whole 4x4x8 slice. The times are simulated.
256 devices in a mesh: section: 4 (over x), seq: 16 (over z, y_hi), tp: 4 (over y_lo, core).
Axes of the slice: x: 4, y: 4 (y_hi: 2, y_lo: 2; y = y_hi * 2 + y_lo), z: 8, core: 2. Of those that a mesh axis runs over, the one named last changes fastest.
Arguments:
- queries: bfloat16 [4, 4096, 8192], P('section', 'seq', 'tp'), may hold values from -135 to 135
- upstream: bfloat16 [4, 4096, 8192], P('section', 'seq', 'tp'), may hold values from -48 to 48
- shared_kv: bfloat16 [2, 4096, 1024], P(None, ('seq', 'tp')), may hold values from -5 to 5
Outputs:
- d_queries: bfloat16 [4, 4096, 8192], P('section', 'seq', 'tp')
- d_shared_kv: float32 [2, 4096, 1024], P(None, ('seq', 'tp'))
All inputs are finite; a program needn't handle non-finite values.
Results may differ from a plain program's by a relative error of at most 0.0098.
Values may be sent and summed in bfloat16 or wider, within the bound.
No kernel may reach another device: no remote copies, remote signals or barrier semaphores. Data moves between devices by JAX's collectives and lax.ppermute only.
A program may use at most 128 MiB of HBM per device.

v0:
```python
import math
import jax
import jax.numpy as jnp
from jax import lax
from jax.sharding import PartitionSpec as P

QH = 64
KVH = 8
HD = 128
WINDOW = 1024


def shifted(value, axis, by):
    peers = lax.axis_size(axis)
    pairs = [(i, i + by) for i in range(peers) if 0 <= i + by < peers]
    return lax.ppermute(value, axis, pairs)


def head_grads(query_block, grad_block, keys_head, values_head, allowed, score_scale):
    scores = (
        jnp.einsum("rgd,ed->gre", query_block, keys_head, preferred_element_type=jnp.float32)
        * score_scale
    )
    masked = jnp.where(allowed[None], scores, -jnp.inf)
    highest = jnp.max(masked, axis=-1, keepdims=True)
    weights = jnp.exp(masked - highest)
    probs = weights / jnp.sum(weights, axis=-1, keepdims=True)
    probs_b = probs.astype(jnp.bfloat16)
    attn_out = jnp.einsum("gre,ed->rgd", probs_b, values_head, preferred_element_type=jnp.float32)
    delta = jnp.sum(grad_block.astype(jnp.float32) * attn_out, axis=-1)
    dprobs = jnp.einsum("rgd,ed->gre", grad_block, values_head, preferred_element_type=jnp.float32)
    dscores = probs * (dprobs - jnp.transpose(delta)[:, :, None])
    dscores_b = dscores.astype(jnp.bfloat16)
    grad_query = (
        jnp.einsum("gre,ed->rgd", dscores_b, keys_head, preferred_element_type=jnp.float32)
        * score_scale
    )
    grad_key = (
        jnp.einsum("gre,rgd->ed", dscores_b, query_block, preferred_element_type=jnp.float32)
        * score_scale
    )
    grad_value = jnp.einsum("gre,rgd->ed", probs_b, grad_block, preferred_element_type=jnp.float32)
    return (grad_query, grad_key, grad_value)


def body(queries, upstream, shared_kv):
    local_kv = lax.all_to_all(shared_kv, "tp", split_axis=2, concat_axis=1, tiled=True)
    tok_rows = local_kv.shape[1]
    kv_cols = local_kv.shape[2]
    head_size = HD
    local_kv_heads = kv_cols // head_size
    group_size = QH // KVH
    block_heads = max(1, group_size // 2)
    span_blocks = WINDOW // tok_rows
    score_scale = 1.0 / math.sqrt(head_size)
    earlier = [shifted(local_kv, "seq", span_blocks - offset) for offset in range(span_blocks)]
    extended = jnp.concatenate(earlier + [local_kv], axis=1)
    ext_rows = extended.shape[1]
    position = lax.axis_index("seq")
    row_ids = lax.broadcasted_iota(jnp.int32, (tok_rows, ext_rows), 0)
    key_ids = lax.broadcasted_iota(jnp.int32, (tok_rows, ext_rows), 1)
    allowed = (
        (key_ids >= row_ids + 1)
        & (key_ids <= row_ids + WINDOW)
        & (position * tok_rows - WINDOW + key_ids >= 0)
    )
    query_heads = queries.reshape(tok_rows, -1, head_size)
    grad_heads = upstream.reshape(tok_rows, -1, head_size)
    query_parts = []
    key_parts = []
    value_parts = []
    for kv_head in range(local_kv_heads):
        keys_head = extended[0, :, kv_head * head_size : (kv_head + 1) * head_size]
        values_head = extended[1, :, kv_head * head_size : (kv_head + 1) * head_size]
        key_total = jnp.zeros((ext_rows, head_size), jnp.float32)
        value_total = jnp.zeros((ext_rows, head_size), jnp.float32)
        for first_head in range(kv_head * group_size, (kv_head + 1) * group_size, block_heads):
            query_block = query_heads[:, first_head : first_head + block_heads]
            grad_block = grad_heads[:, first_head : first_head + block_heads]
            grad_query, grad_key, grad_value = head_grads(
                query_block, grad_block, keys_head, values_head, allowed, score_scale
            )
            query_parts.append(grad_query)
            key_total = key_total + grad_key
            value_total = value_total + grad_value
        key_parts.append(key_total)
        value_parts.append(value_total)
    d_queries = jnp.concatenate(query_parts, axis=1).reshape(1, tok_rows, -1).astype(jnp.bfloat16)
    grad_ext = jnp.stack([jnp.concatenate(key_parts, axis=1), jnp.concatenate(value_parts, axis=1)])
    own_rows = grad_ext[:, span_blocks * tok_rows :, :]
    for offset in range(span_blocks):
        own_rows = own_rows + shifted(
            grad_ext[:, offset * tok_rows : (offset + 1) * tok_rows, :].astype(jnp.bfloat16),
            "seq",
            offset - span_blocks,
        ).astype(jnp.float32)
    summed = lax.psum(own_rows, "section")
    d_shared_kv = lax.all_to_all(summed, "tp", split_axis=1, concat_axis=2, tiled=True)
    return (d_queries, d_shared_kv)


def solution(mesh):
    in_specs = (P("section", "seq", "tp"), P("section", "seq", "tp"), P(None, ("seq", "tp"), None))
    out_specs = (P("section", "seq", "tp"), P(None, ("seq", "tp"), None))
    return jax.shard_map(body, mesh=mesh, in_specs=in_specs, out_specs=out_specs, check_vma=False)
```

profile of v0, /device:TPU:1, one launch (start us, length us, event | category | flops | bytes accessed | tf_op | source)
XLA Modules:
  0.0 228.5 jit_solution(4104117547018688944)
XLA Ops:
  7.2 1.4 copy.143
  8.5 1.1 reshape.105
  9.6 6.6 %all-to-all-start = ((bf16[4,2,16384]{2,1,0:T(2,128)(2,1)}), bf16[4,2,16384]{2,1,0:T(2,128)(2,1)S(1)}, u32[]{:S(2)}, u32[]{:S(2)}) async-start(bf16[4,2,16384]{2,1,0:T(2,128)(2,1)} %reshape.105), calls=%async_computation | async-start | bytes 524288 | tf_op jit(solution)/shard_map/all_to_all | solution.py:47
  16.2 5.0 %all-to-all-done = bf16[4,2,16384]{2,1,0:T(2,128)(2,1)S(1)} async-done(((bf16[4,2,16384]{2,1,0:T(2,128)(2,1)}), bf16[4,2,16384]{2,1,0:T(2,128)(2,1)S(1)}, u32[]{:S(2)}, u32[]{:S(2)}) %all-to-all-start) | async-done | bytes 262176 | tf_op jit(solution)/shard_map/all_to_all | solution.py:47
  21.6 1.0 copy.144
  22.6 3.9 %collective-permute-start = (bf16[2,256,256]{2,1,0:T(8,128)(2,1)}, bf16[2,256,256]{2,1,0:T(8,128)(2,1)}, u32[]{:S(2)}, u32[]{:S(2)}) collective-permute-start(bf16[2,256,256]{2,1,0:T(8,128)(2,1)} %bitcast.2), channel_id=1, source_target_pairs={{0,16},{4,20},{8,24},{12,28},{16,32},{20,36},{24,40},{28,44},{32,4... | collective-permute-start | bytes 786440 | tf_op jit(solution)/shard_map/ppermute | solution.py:16
  26.5 1.1 fusion.28
  28.2 4.3 %collective-permute-start.2 = (bf16[2,256,256]{2,1,0:T(8,128)(2,1)}, bf16[2,256,256]{2,1,0:T(8,128)(2,1)}, u32[]{:S(2)}, u32[]{:S(2)}) collective-permute-start(bf16[2,256,256]{2,1,0:T(8,128)(2,1)} %bitcast.2), channel_id=1, source_target_pairs={{0,8},{4,12},{8,16},{12,20},{16,24},{20,28},{24,32},{28,36},{32,40... | collective-permute-start | bytes 786440 | tf_op jit(solution)/shard_map/ppermute | solution.py:16
  32.4 6.7 %collective-permute-start.1 = (bf16[2,256,256]{2,1,0:T(8,128)(2,1)}, bf16[2,256,256]{2,1,0:T(8,128)(2,1)}, u32[]{:S(2)}, u32[]{:S(2)}) collective-permute-start(bf16[2,256,256]{2,1,0:T(8,128)(2,1)} %bitcast.2), channel_id=1, source_target_pairs={{0,12},{4,16},{8,20},{12,24},{16,28},{20,32},{24,36},{28,40},{32,4... | collective-permute-start | bytes 786440 | tf_op jit(solution)/shard_map/ppermute | solution.py:16
  39.2 1.5 copy.145
  40.7 1.0 copy.240
  41.7 0.9 copy.244
  42.6 0.9 copy.242
  43.5 0.8 copy.246
  44.3 2.6 %collective-permute-start.3 = (bf16[2,256,256]{2,1,0:T(8,128)(2,1)}, bf16[2,256,256]{2,1,0:T(8,128)(2,1)S(1)}, u32[]{:S(2)}, u32[]{:S(2)}) collective-permute-start(bf16[2,256,256]{2,1,0:T(8,128)(2,1)} %bitcast.2), channel_id=1, source_target_pairs={{0,4},{4,8},{8,12},{12,16},{16,20},{20,24},{24,28},{28,32},{32,36}... | collective-permute-start | bytes 786440 | tf_op jit(solution)/shard_map/ppermute | solution.py:16
  46.9 1.0 constant_dynamic-update-slice_fusion.4
  47.9 1.0 constant_dynamic-update-slice_fusion.3
  48.9 1.0 constant_dynamic-update-slice_fusion.2
  49.9 1.0 collective-permute-done.3
  50.9 1.0 constant_dynamic-update-slice_fusion
  51.9 5.3 %exponential_reduce_fusion.3 = (f32[4,256]{1,0:T(4,128)S(1)}, f32[4,256,1280]{1,2,0:T(8,128)}) fusion(pred[256,1280]{0,1:T(8,128)(4,1)} %fusion.28, bf16[256,16,128]{0,2,1:T(8,128)(2,1)S(1)} %bitcast.227, bf16[2,1280,256]{2,1,0:T(8,128)(2,1)S(1)} %constant_dynamic-update-slice_fusion), kind=kOutput, calls=%fused_computation.31 | convolution fusion | flops 340788480 | bytes 6164480 | tf_op jit(solution)/shard_map/sub | solution.py:26
  57.1 5.1 %exponential_reduce_fusion.1 = (f32[4,256]{1,0:T(4,128)S(1)}, f32[4,256,1280]{1,2,0:T(8,128)}) fusion(pred[256,1280]{0,1:T(8,128)(4,1)} %fusion.28, bf16[256,16,128]{0,2,1:T(8,128)(2,1)S(1)} %bitcast.228, bf16[2,1280,256]{2,1,0:T(8,128)(2,1)S(1)} %constant_dynamic-update-slice_fusion), kind=kOutput, calls=%fused_computation.27 | convolution fusion | flops 340788480 | bytes 6164480 | tf_op jit(solution)/shard_map/sub | solution.py:26
  62.3 5.1 %exponential_reduce_fusion.2 = (f32[4,256]{1,0:T(4,128)S(1)}, f32[4,256,1280]{1,2,0:T(8,128)}) fusion(pred[256,1280]{0,1:T(8,128)(4,1)} %fusion.28, bf16[256,16,128]{0,2,1:T(8,128)(2,1)S(1)} %bitcast.229, bf16[2,1280,256]{2,1,0:T(8,128)(2,1)S(1)} %constant_dynamic-update-slice_fusion), kind=kOutput, calls=%fused_computation.29 | convolution fusion | flops 340788480 | bytes 6164480 | tf_op jit(solution)/shard_map/sub | solution.py:26
  67.4 5.1 %exponential_reduce_fusion = (f32[4,256]{1,0:T(4,128)S(1)}, f32[4,256,1280]{1,2,0:T(8,128)}) fusion(pred[256,1280]{0,1:T(8,128)(4,1)} %fusion.28, bf16[256,16,128]{0,2,1:T(8,128)(2,1)S(1)} %bitcast.230, bf16[2,1280,256]{2,1,0:T(8,128)(2,1)S(1)} %constant_dynamic-update-slice_fusion), kind=kOutput, calls=%fused_computation.25 | convolution fusion | flops 340788480 | bytes 6164480 | tf_op jit(solution)/shard_map/sub | solution.py:26
  72.5 4.0 %fusion.23 = bf16[4,256,1280]{1,2,0:T(8,128)(2,1)S(1)} fusion(f32[4,256]{1,0:T(4,128)S(1)} %get-tuple-element.24, f32[4,256,1280]{1,2,0:T(8,128)} %get-tuple-element.25), kind=kLoop, calls=%fused_computation.50 | loop fusion | flops 2621440 | bytes 7868416 | tf_op jit(solution)/shard_map/convert_element_type | solution.py:28
  76.5 1.0 convolution_bitcast_fusion.3
  77.5 1.3 fusion.37
  78.8 1.1 fusion.15
  79.9 1.0 convolution_bitcast_fusion.7
  81.2 1.6 fusion.25
  82.9 1.0 convolution_bitcast_fusion.1
  83.9 1.3 fusion.39
  85.2 1.1 fusion.11
  86.3 1.0 convolution_bitcast_fusion.5
  87.3 0.6 copy-done.2
  87.9 0.7 slice-done.3
  88.6 1.4 fusion.24
  90.0 1.3 fusion.38
  91.3 1.0 fusion.18
  92.3 1.1 fusion.13
  93.5 1.2 slice-done
  94.7 1.0 slice-done.1
  95.7 1.4 fusion.26
  97.2 1.3 fusion.40
  98.5 1.0 fusion.17
  99.8 2.5 %fusion.9 = bf16[4,256,1280]{1,2,0:T(8,128)(2,1)S(1)} fusion(f32[4,256]{1,0:T(4,128)S(1)} %bitcast.240, f32[4,256]{1,0:T(4,128)S(1)} %get-tuple-element.18, f32[4,256,1280]{1,2,0:T(8,128)S(1)} %bitcast.220, bf16[2,1280,256]{2,1,0:T(8,128)(2,1)S(1)} %copy-done.5, bf16[256,16,128]{0,2,1:T(8,128)(2,1)} %bitcast.218), kind=kOutput, calls=%fused_computation.10 | convolution fusion | flops 340787200 | bytes 8462336 | tf_op jit(solution)/shard_map/rgd,ed->gre/dot_general | solution.py:31
  102.3 1.0 fusion.22
  103.4 1.0 fusion.20
  104.7 1.3 collective-permute-start.4
  106.0 1.3 collective-permute-start.7
  107.3 1.3 collective-permute-start.6
  108.6 1.3 collective-permute-start.5
  110.5 22.5 %collective-permute-done.4 = bf16[2,256,256]{1,2,0:T(8,128)(2,1)S(1)} collective-permute-done((bf16[2,256,256]{1,2,0:T(8,128)(2,1)S(1)}, bf16[2,256,256]{1,2,0:T(8,128)(2,1)S(1)}, u32[]{:S(2)}, u32[]{:S(2)}) %collective-permute-start.4) | collective-permute-done | bytes 262176 | tf_op jit(solution)/shard_map/ppermute | solution.py:16
  133.0 6.1 %collective-permute-done.5 = bf16[2,256,256]{1,2,0:T(8,128)(2,1)S(1)} collective-permute-done((bf16[2,256,256]{1,2,0:T(8,128)(2,1)S(1)}, bf16[2,256,256]{1,2,0:T(8,128)(2,1)S(1)}, u32[]{:S(2)}, u32[]{:S(2)}) %collective-permute-start.5) | collective-permute-done | bytes 262176 | tf_op jit(solution)/shard_map/ppermute | solution.py:16
  139.1 1.0 fusion.49
  140.1 3.2 %fusion.42 = bf16[256,4,128]{0,2,1:T(8,128)(2,1)} fusion(bf16[4,256,1280]{1,2,0:T(8,128)(2,1)} %copy-done.2, bf16[2,1280,256]{2,1,0:T(8,128)(2,1)} %copy-done.4), kind=kOutput, calls=%fused_computation.81 | convolution fusion | flops 335806464 | bytes 3211264 | tf_op jit(solution)/shard_map/gre,ed->rgd/dot_general | solution.py:35
  143.3 2.2 fusion.43
  145.5 59.1 %all-reduce.2.cloned.1.call-done = f32[2,256,256]{1,2,0:T(8,128)} async-done(((f32[2,256,256]{1,2,0:T(8,128)}), f32[2,256,256]{1,2,0:T(8,128)}) %all-reduce.2.cloned.1.call-update) | async-done | bytes 524304 | tf_op jit(solution)/shard_map/psum | solution.py:97
  204.6 2.0 copy.191
  206.6 6.3 %all-to-all-start.1 = ((f32[2,256,256]{2,0,1:T(2,128)}), f32[2,256,256]{2,0,1:T(2,128)S(1)}, u32[]{:S(2)}, u32[]{:S(2)}) async-start(f32[2,256,256]{2,0,1:T(2,128)} %copy.191), calls=%async_computation.1 | async-start | bytes 1048576 | tf_op jit(solution)/shard_map/all_to_all | solution.py:98
  213.0 1.6 fusion.41
  214.7 1.4 copy.194
  216.1 4.7 %all-to-all-done.1 = f32[2,256,256]{2,0,1:T(2,128)S(1)} async-done(((f32[2,256,256]{2,0,1:T(2,128)}), f32[2,256,256]{2,0,1:T(2,128)S(1)}, u32[]{:S(2)}, u32[]{:S(2)}) %all-to-all-start.1) | async-done | bytes 524320 | tf_op jit(solution)/shard_map/all_to_all | solution.py:98
  220.8 0.8 copy.247
  (66 shorter events, 2.9 us)
Async XLA Ops:
  7.2 20.5 %copy-start.12 = (bf16[1,256,2048]{2,1,0:T(8,128)(2,1)S(1)}, bf16[1,256,2048]{2,1,0:T(8,128)(2,1)}, u32[]{:S(2)}) copy-start(bf16[1,256,2048]{2,1,0:T(8,128)(2,1)} %param.4) | copy-start | bytes 3145732
  9.6 11.6 %all-to-all-start = ((bf16[4,2,16384]{2,1,0:T(2,128)(2,1)}), bf16[4,2,16384]{2,1,0:T(2,128)(2,1)S(1)}, u32[]{:S(2)}, u32[]{:S(2)}) async-start(bf16[4,2,16384]{2,1,0:T(2,128)(2,1)} %reshape.105), calls=%async_computation | async-start | bytes 524288 | tf_op jit(solution)/shard_map/all_to_all | solution.py:47
  16.2 188.4 %all-reduce.2.cloned.1.call-start = ((), (), s32[]{:S(2)}) async-start(), calls=%async_computation.2 | async-start | bytes 1048576 | tf_op jit(solution)/shard_map/psum | solution.py:97
  22.6 24.3 %collective-permute-start = (bf16[2,256,256]{2,1,0:T(8,128)(2,1)}, bf16[2,256,256]{2,1,0:T(8,128)(2,1)}, u32[]{:S(2)}, u32[]{:S(2)}) collective-permute-start(bf16[2,256,256]{2,1,0:T(8,128)(2,1)} %bitcast.2), channel_id=1, source_target_pairs={{0,16},{4,20},{8,24},{12,28},{16,32},{20,36},{24,40},{28,44},{32,4... | collective-permute-start | bytes 786440 | tf_op jit(solution)/shard_map/ppermute | solution.py:16
  28.2 70.3 %copy-start.3 = (bf16[1,256,2048]{1,2,0:T(8,128)(2,1)}, bf16[1,256,2048]{1,2,0:T(8,128)(2,1)S(1)}, u32[]{:S(2)}) copy-start(bf16[1,256,2048]{1,2,0:T(8,128)(2,1)S(1)} %copy.147) | copy-start | bytes 3145732
  28.2 20.7 %collective-permute-start.2 = (bf16[2,256,256]{2,1,0:T(8,128)(2,1)}, bf16[2,256,256]{2,1,0:T(8,128)(2,1)}, u32[]{:S(2)}, u32[]{:S(2)}) collective-permute-start(bf16[2,256,256]{2,1,0:T(8,128)(2,1)} %bitcast.2), channel_id=1, source_target_pairs={{0,8},{4,12},{8,16},{12,20},{16,24},{20,28},{24,32},{28,36},{32,40... | collective-permute-start | bytes 786440 | tf_op jit(solution)/shard_map/ppermute | solution.py:16
  32.4 15.5 %collective-permute-start.1 = (bf16[2,256,256]{2,1,0:T(8,128)(2,1)}, bf16[2,256,256]{2,1,0:T(8,128)(2,1)}, u32[]{:S(2)}, u32[]{:S(2)}) collective-permute-start(bf16[2,256,256]{2,1,0:T(8,128)(2,1)} %bitcast.2), channel_id=1, source_target_pairs={{0,12},{4,16},{8,20},{12,24},{16,28},{20,32},{24,36},{28,40},{32,4... | collective-permute-start | bytes 786440 | tf_op jit(solution)/shard_map/ppermute | solution.py:16
  40.7 45.6 %copy-start.6 = (bf16[1,256,2048]{1,2,0:T(8,128)(2,1)}, bf16[1,256,2048]{1,2,0:T(8,128)(2,1)S(1)}, u32[]{:S(2)}) copy-start(bf16[1,256,2048]{1,2,0:T(8,128)(2,1)S(1)} %copy.145) | copy-start | bytes 3145732
  44.3 6.6 %collective-permute-start.3 = (bf16[2,256,256]{2,1,0:T(8,128)(2,1)}, bf16[2,256,256]{2,1,0:T(8,128)(2,1)S(1)}, u32[]{:S(2)}, u32[]{:S(2)}) collective-permute-start(bf16[2,256,256]{2,1,0:T(8,128)(2,1)} %bitcast.2), channel_id=1, source_target_pairs={{0,4},{4,8},{8,12},{12,16},{16,20},{20,24},{24,28},{28,32},{32,36}... | collective-permute-start | bytes 786440 | tf_op jit(solution)/shard_map/ppermute | solution.py:16
  51.9 45.3 %copy-start.4 = (bf16[2,1280,256]{2,1,0:T(8,128)(2,1)}, bf16[2,1280,256]{2,1,0:T(8,128)(2,1)S(1)}, u32[]{:S(2)}) copy-start(bf16[2,1280,256]{2,1,0:T(8,128)(2,1)S(1)} %constant_dynamic-update-slice_fusion) | copy-start | bytes 3932164
  72.5 6.3 %slice-start.6 = ((s8[5242880]{0:T(1024)(128)(4,1)}), s8[4194304]{0:T(1024)(128)(4,1)S(1)}, s32[]{:S(2)}) async-start(s8[5242880]{0:T(1024)(128)(4,1)} %bitcast.225), calls=%async_computation.9 | async-start | bytes 8388608
  76.5 1.0 copy-start.11
  76.5 2.3 %slice-start.7 = ((s8[5242880]{0:T(1024)(128)(4,1)}), s8[1048576]{0:T(1024)(128)(4,1)S(1)}, s32[]{:S(2)}) async-start(s8[5242880]{0:T(1024)(128)(4,1)} %bitcast.225), calls=%async_computation.10 | async-start | bytes 2097152
  78.8 2.2 slice-start.4
  78.8 2.5 %slice-start.5 = ((s8[5242880]{0:T(1024)(128)(4,1)}), s8[1048576]{0:T(1024)(128)(4,1)S(1)}, s32[]{:S(2)}) async-start(s8[5242880]{0:T(1024)(128)(4,1)} %bitcast.223), calls=%async_computation.8 | async-start | bytes 2097152
  82.9 1.0 copy-start.10
  85.2 2.7 %slice-start.2 = ((s8[5242880]{0:T(1024)(128)(4,1)}), s8[4194304]{0:T(1024)(128)(4,1)S(1)}, s32[]{:S(2)}) async-start(s8[5242880]{0:T(1024)(128)(4,1)} %bitcast.221), calls=%async_computation.5 | async-start | bytes 8388608
  85.2 3.4 %slice-start.3 = ((s8[5242880]{0:T(1024)(128)(4,1)}), s8[1048576]{0:T(1024)(128)(4,1)S(1)}, s32[]{:S(2)}) async-start(s8[5242880]{0:T(1024)(128)(4,1)} %bitcast.221), calls=%async_computation.6 | async-start | bytes 2097152
  86.3 1.6 copy-start.2
  88.6 1.4 copy-start.9
  92.3 2.4 %slice-start = ((s8[5242880]{0:T(1024)(128)(4,1)}), s8[4194304]{0:T(1024)(128)(4,1)S(1)}, s32[]{:S(2)}) async-start(s8[5242880]{0:T(1024)(128)(4,1)} %bitcast.219), calls=%async_computation.3 | async-start | bytes 8388608
  92.3 3.4 %slice-start.1 = ((s8[5242880]{0:T(1024)(128)(4,1)}), s8[1048576]{0:T(1024)(128)(4,1)S(1)}, s32[]{:S(2)}) async-start(s8[5242880]{0:T(1024)(128)(4,1)} %bitcast.219), calls=%async_computation.4 | async-start | bytes 2097152
  93.5 8.8 %copy-start = (bf16[4,256,1280]{1,2,0:T(8,128)(2,1)}, bf16[4,256,1280]{1,2,0:T(8,128)(2,1)S(1)}, u32[]{:S(2)}) copy-start(bf16[4,256,1280]{1,2,0:T(8,128)(2,1)S(1)} %fusion.13) | copy-start | bytes 7864324
  95.7 1.4 copy-start.8
  98.5 1.3 copy-start.5
  99.8 2.5 %copy-start.7 = (bf16[1,256,2048]{1,2,0:T(8,128)(2,1)S(1)}, bf16[1,256,2048]{1,2,0:T(8,128)(2,1)}, u32[]{:S(2)}) copy-start(bf16[1,256,2048]{1,2,0:T(8,128)(2,1)} %copy-done.6) | copy-start | bytes 3145732
  104.7 28.2 %collective-permute-start.4 = (bf16[2,256,256]{1,2,0:T(8,128)(2,1)S(1)}, bf16[2,256,256]{1,2,0:T(8,128)(2,1)S(1)}, u32[]{:S(2)}, u32[]{:S(2)}) collective-permute-start(bf16[2,256,256]{1,2,0:T(8,128)(2,1)S(1)} %get-tuple-element.10), channel_id=1, source_target_pairs={{16,0},{20,4},{24,8},{28,12},{32,16},{36,20},{40,24},{44,28},{48,3... | collective-permute-start | bytes 786440 | tf_op jit(solution)/shard_map/ppermute | solution.py:16
  106.0 26.9 %collective-permute-start.7 = (bf16[2,256,256]{1,2,0:T(8,128)(2,1)S(1)}, bf16[2,256,256]{1,2,0:T(8,128)(2,1)S(1)}, u32[]{:S(2)}, u32[]{:S(2)}) collective-permute-start(bf16[2,256,256]{1,2,0:T(8,128)(2,1)S(1)} %get-tuple-element.11), channel_id=1, source_target_pairs={{4,0},{8,4},{12,8},{16,12},{20,16},{24,20},{28,24},{32,28},{36,32}... | collective-permute-start | bytes 786440 | tf_op jit(solution)/shard_map/ppermute | solution.py:16
  107.3 25.6 %collective-permute-start.6 = (bf16[2,256,256]{1,2,0:T(8,128)(2,1)S(1)}, bf16[2,256,256]{1,2,0:T(8,128)(2,1)S(1)}, u32[]{:S(2)}, u32[]{:S(2)}) collective-permute-start(bf16[2,256,256]{1,2,0:T(8,128)(2,1)S(1)} %get-tuple-element.12), channel_id=1, source_target_pairs={{8,0},{12,4},{16,8},{20,12},{24,16},{28,20},{32,24},{36,28},{40,32... | collective-permute-start | bytes 786440 | tf_op jit(solution)/shard_map/ppermute | solution.py:16
  108.6 30.4 %collective-permute-start.5 = (bf16[2,256,256]{1,2,0:T(8,128)(2,1)S(1)}, bf16[2,256,256]{1,2,0:T(8,128)(2,1)S(1)}, u32[]{:S(2)}, u32[]{:S(2)}) collective-permute-start(bf16[2,256,256]{1,2,0:T(8,128)(2,1)S(1)} %get-tuple-element.13), channel_id=1, source_target_pairs={{12,0},{16,4},{20,8},{24,12},{28,16},{32,20},{36,24},{40,28},{44,3... | collective-permute-start | bytes 786440 | tf_op jit(solution)/shard_map/ppermute | solution.py:16
  140.1 3.3 %copy-start.1 = (bf16[4,256,1280]{1,2,0:T(8,128)(2,1)S(1)}, bf16[4,256,1280]{1,2,0:T(8,128)(2,1)}, u32[]{:S(2)}) copy-start(bf16[4,256,1280]{1,2,0:T(8,128)(2,1)} %copy-done) | copy-start | bytes 7864324
  206.6 14.2 %all-to-all-start.1 = ((f32[2,256,256]{2,0,1:T(2,128)}), f32[2,256,256]{2,0,1:T(2,128)S(1)}, u32[]{:S(2)}, u32[]{:S(2)}) async-start(f32[2,256,256]{2,0,1:T(2,128)} %copy.191), calls=%async_computation.1 | async-start | bytes 1048576 | tf_op jit(solution)/shard_map/all_to_all | solution.py:98
  213.0 1.6 copy-start.13
  213.0 1.6 copy-start.14
Sparse Core Ops, SparseCore 0:
  140.2 64.3 all-reduce.1
where the time goes:
time: 229 us
  waiting for transfers between devices  98.4 us (43%)
  matrix products  47 us (21%)
  starting transfers between devices  35.5 us (16%)
  local copies, waits for them, and re-layouts  22.1 us (10%)
  between operations  14.6 us (6%)
  other arithmetic  11 us (5%)
    psum x1, waiting for transfers between devices, body(): summed = lax.psum(own_rows, 'section')  59.1 us
    ppermute x8, waiting for transfers between devices, shifted(): return lax.ppermute(value, axis, pairs)  29.6 us
    ppermute x8, starting transfers between devices, shifted(): return lax.ppermute(value, axis, pairs)  22.6 us
    sub x4, matrix products, head_grads(): weights = jnp.exp(masked - highest)  20.6 us
    unnamed x61, local copies, waits for them, and re-layouts  17.1 us
    convert_element_type x4, other arithmetic, head_grads(): probs_b = probs.astype(jnp.bfloat16)  8.43 us
    dot_general x4, matrix products, head_grads(): jnp.einsum('gre,ed->rgd', dscores_b, keys_head, preferred_element_type=jn...  7.58 us
    all_to_all x1, starting transfers between devices, body(): lax.all_to_all(shared_kv, 'tp', split_axis=2, concat_axis=1, tiled=True)  6.57 us
  transfers between devices with their start and end apart: 11, of which 6 were waited for; matrix products, arithmetic and copies ran while one was open for 8% of the time, Pallas kernels for 0%

commit v1 on v0

--- a/solution.py
+++ b/solution.py
@@ -94,7 +94,7 @@
             "seq",
             offset - span_blocks,
         ).astype(jnp.float32)
-    summed = lax.psum(own_rows, "section")
+    summed = jnp.sum(jax.lax.all_gather(own_rows, "section"), axis=0)
     d_shared_kv = lax.all_to_all(summed, "tp", split_axis=1, concat_axis=2, tiled=True)
     return (d_queries, d_shared_kv)
 

time: 229 us -> 216 us (0.943)
  waiting for transfers between devices: 98.4 us -> 83.7 us
    psum x1 -> x0, waiting for transfers between devices: 59.1 us -> none  [body(): summed = lax.psum(own_rows, 'section')]
    all_gather x0 -> x1, waiting for transfers between devices: none -> 43.8 us  [body(): summed = jnp.sum(jax.lax.all_gather(own_rows, 'section'), axis=0)]
  transfers between devices with their start and end apart: 11 -> 11, of which waited for: 6 -> 6; matrix products, arithmetic and copies ran while one was open for 8% -> 10% of each run, Pallas kernels for 0% -> 0%
where the time goes in v1:
time: 216 us
  waiting for transfers between devices  83.7 us (39%)
  matrix products  48.9 us (23%)
  starting transfers between devices  33.5 us (16%)
  local copies, waits for them, and re-layouts  22.8 us (11%)
  between operations  14.6 us (7%)
  other arithmetic  12 us (6%)
    all_gather x1, waiting for transfers between devices, body(): summed = jnp.sum(jax.lax.all_gather(own_rows, 'section'), axis=0)  43.8 us
    ppermute x8, waiting for transfers between devices, shifted(): return lax.ppermute(value, axis, pairs)  30.2 us
    ppermute x8, starting transfers between devices, shifted(): return lax.ppermute(value, axis, pairs)  22.6 us
    sub x4, matrix products, head_grads(): weights = jnp.exp(masked - highest)  20.6 us
    unnamed x61, local copies, waits for them, and re-layouts  17.7 us
    dot_general x4, matrix products, head_grads(): jnp.einsum('gre,ed->rgd', dscores_b, keys_head, preferred_element_type=jn...  9.44 us
    convert_element_type x4, other arithmetic, head_grads(): probs_b = probs.astype(jnp.bfloat16)  8.43 us
    all_to_all x1, starting transfers between devices, body(): lax.all_to_all(shared_kv, 'tp', split_axis=2, concat_axis=1, tiled=True)  6.57 us
  transfers between devices with their start and end apart: 11, of which 6 were waited for; matrix products, arithmetic and copies ran while one was open for 10% of the time, Pallas kernels for 0%

profile of v1, /device:TPU:1, one launch (start us, length us, event | category | flops | bytes accessed | tf_op | source)
XLA Modules:
  0.0 215.5 jit_solution(13922902531498575796)
XLA Ops:
  7.2 1.4 copy.140
  8.5 1.1 reshape.106
  9.6 6.6 %all-to-all-start = ((bf16[4,2,16384]{2,1,0:T(2,128)(2,1)}), bf16[4,2,16384]{2,1,0:T(2,128)(2,1)S(1)}, u32[]{:S(2)}, u32[]{:S(2)}) async-start(bf16[4,2,16384]{2,1,0:T(2,128)(2,1)} %reshape.106), calls=%async_computation | async-start | bytes 524288 | tf_op jit(solution)/shard_map/all_to_all | solution.py:47
  16.2 5.0 %all-to-all-done = bf16[4,2,16384]{2,1,0:T(2,128)(2,1)S(1)} async-done(((bf16[4,2,16384]{2,1,0:T(2,128)(2,1)}), bf16[4,2,16384]{2,1,0:T(2,128)(2,1)S(1)}, u32[]{:S(2)}, u32[]{:S(2)}) %all-to-all-start) | async-done | bytes 262176 | tf_op jit(solution)/shard_map/all_to_all | solution.py:47
  21.6 1.0 copy.141
  22.6 3.9 %collective-permute-start = (bf16[2,256,256]{2,1,0:T(8,128)(2,1)}, bf16[2,256,256]{2,1,0:T(8,128)(2,1)}, u32[]{:S(2)}, u32[]{:S(2)}) collective-permute-start(bf16[2,256,256]{2,1,0:T(8,128)(2,1)} %bitcast.2), channel_id=1, source_target_pairs={{0,16},{4,20},{8,24},{12,28},{16,32},{20,36},{24,40},{28,44},{32,4... | collective-permute-start | bytes 786440 | tf_op jit(solution)/shard_map/ppermute | solution.py:16
  26.5 1.1 fusion.28
  28.2 4.3 %collective-permute-start.2 = (bf16[2,256,256]{2,1,0:T(8,128)(2,1)}, bf16[2,256,256]{2,1,0:T(8,128)(2,1)}, u32[]{:S(2)}, u32[]{:S(2)}) collective-permute-start(bf16[2,256,256]{2,1,0:T(8,128)(2,1)} %bitcast.2), channel_id=1, source_target_pairs={{0,8},{4,12},{8,16},{12,20},{16,24},{20,28},{24,32},{28,36},{32,40... | collective-permute-start | bytes 786440 | tf_op jit(solution)/shard_map/ppermute | solution.py:16
  32.4 6.7 %collective-permute-start.1 = (bf16[2,256,256]{2,1,0:T(8,128)(2,1)}, bf16[2,256,256]{2,1,0:T(8,128)(2,1)}, u32[]{:S(2)}, u32[]{:S(2)}) collective-permute-start(bf16[2,256,256]{2,1,0:T(8,128)(2,1)} %bitcast.2), channel_id=1, source_target_pairs={{0,12},{4,16},{8,20},{12,24},{16,28},{20,32},{24,36},{28,40},{32,4... | collective-permute-start | bytes 786440 | tf_op jit(solution)/shard_map/ppermute | solution.py:16
  39.2 1.5 copy.142
  40.7 1.0 copy.240
  41.7 0.9 copy.244
  42.6 0.9 copy.242
  43.5 0.8 copy.246
  44.3 2.6 %collective-permute-start.3 = (bf16[2,256,256]{2,1,0:T(8,128)(2,1)}, bf16[2,256,256]{2,1,0:T(8,128)(2,1)S(1)}, u32[]{:S(2)}, u32[]{:S(2)}) collective-permute-start(bf16[2,256,256]{2,1,0:T(8,128)(2,1)} %bitcast.2), channel_id=1, source_target_pairs={{0,4},{4,8},{8,12},{12,16},{16,20},{20,24},{24,28},{28,32},{32,36}... | collective-permute-start | bytes 786440 | tf_op jit(solution)/shard_map/ppermute | solution.py:16
  46.9 1.0 constant_dynamic-update-slice_fusion.4
  47.9 1.0 constant_dynamic-update-slice_fusion.3
  48.9 1.0 constant_dynamic-update-slice_fusion.2
  49.9 1.0 collective-permute-done.3
  50.9 1.0 constant_dynamic-update-slice_fusion
  51.9 5.3 %exponential_reduce_fusion.3 = (f32[4,256]{1,0:T(4,128)S(1)}, f32[4,256,1280]{1,2,0:T(8,128)}) fusion(pred[256,1280]{0,1:T(8,128)(4,1)} %fusion.28, bf16[256,16,128]{0,2,1:T(8,128)(2,1)S(1)} %bitcast.228, bf16[2,1280,256]{2,1,0:T(8,128)(2,1)S(1)} %constant_dynamic-update-slice_fusion), kind=kOutput, calls=%fused_computation.31 | convolution fusion | flops 340788480 | bytes 6164480 | tf_op jit(solution)/shard_map/sub | solution.py:26
  57.1 5.1 %exponential_reduce_fusion.1 = (f32[4,256]{1,0:T(4,128)S(1)}, f32[4,256,1280]{1,2,0:T(8,128)}) fusion(pred[256,1280]{0,1:T(8,128)(4,1)} %fusion.28, bf16[256,16,128]{0,2,1:T(8,128)(2,1)S(1)} %bitcast.229, bf16[2,1280,256]{2,1,0:T(8,128)(2,1)S(1)} %constant_dynamic-update-slice_fusion), kind=kOutput, calls=%fused_computation.27 | convolution fusion | flops 340788480 | bytes 6164480 | tf_op jit(solution)/shard_map/sub | solution.py:26
  62.3 5.1 %exponential_reduce_fusion.2 = (f32[4,256]{1,0:T(4,128)S(1)}, f32[4,256,1280]{1,2,0:T(8,128)}) fusion(pred[256,1280]{0,1:T(8,128)(4,1)} %fusion.28, bf16[256,16,128]{0,2,1:T(8,128)(2,1)S(1)} %bitcast.230, bf16[2,1280,256]{2,1,0:T(8,128)(2,1)S(1)} %constant_dynamic-update-slice_fusion), kind=kOutput, calls=%fused_computation.29 | convolution fusion | flops 340788480 | bytes 6164480 | tf_op jit(solution)/shard_map/sub | solution.py:26
  67.4 5.1 %exponential_reduce_fusion = (f32[4,256]{1,0:T(4,128)S(1)}, f32[4,256,1280]{1,2,0:T(8,128)}) fusion(pred[256,1280]{0,1:T(8,128)(4,1)} %fusion.28, bf16[256,16,128]{0,2,1:T(8,128)(2,1)S(1)} %bitcast.231, bf16[2,1280,256]{2,1,0:T(8,128)(2,1)S(1)} %constant_dynamic-update-slice_fusion), kind=kOutput, calls=%fused_computation.25 | convolution fusion | flops 340788480 | bytes 6164480 | tf_op jit(solution)/shard_map/sub | solution.py:26
  72.5 4.0 %fusion.23 = bf16[4,256,1280]{1,2,0:T(8,128)(2,1)S(1)} fusion(f32[4,256]{1,0:T(4,128)S(1)} %get-tuple-element.24, f32[4,256,1280]{1,2,0:T(8,128)} %get-tuple-element.25), kind=kLoop, calls=%fused_computation.50 | loop fusion | flops 2621440 | bytes 7868416 | tf_op jit(solution)/shard_map/convert_element_type | solution.py:28
  76.5 1.0 convolution_bitcast_fusion.3
  77.5 1.3 fusion.37
  78.8 1.1 fusion.15
  79.9 1.0 convolution_bitcast_fusion.7
  82.2 1.6 fusion.25
  83.8 1.0 convolution_bitcast_fusion.1
  84.8 1.3 fusion.39
  86.1 1.1 fusion.11
  87.3 1.0 convolution_bitcast_fusion.5
  89.5 1.4 fusion.24
  91.0 1.3 fusion.38
  92.2 1.0 fusion.18
  93.2 1.1 fusion.13
  94.4 1.2 slice-done
  95.6 1.0 slice-done.1
  96.7 1.4 fusion.26
  98.1 1.3 fusion.40
  99.4 1.0 fusion.17
  100.4 2.5 %fusion.9 = bf16[4,256,1280]{1,2,0:T(8,128)(2,1)S(1)} fusion(f32[4,256]{1,0:T(4,128)S(1)} %bitcast.242, f32[4,256]{1,0:T(4,128)S(1)} %get-tuple-element.18, f32[4,256,1280]{1,2,0:T(8,128)S(1)} %bitcast.221, bf16[2,1280,256]{2,1,0:T(8,128)(2,1)} %copy-done.5, bf16[256,16,128]{0,2,1:T(8,128)(2,1)} %bitcast.219), kind=kOutput, calls=%fused_computation.10 | convolution fusion | flops 340787200 | bytes 8462336 | tf_op jit(solution)/shard_map/rgd,ed->gre/dot_general | solution.py:31
  102.9 1.0 fusion.22
  104.0 1.0 fusion.20
  105.4 1.3 collective-permute-start.4
  106.7 1.3 collective-permute-start.7
  108.0 1.3 collective-permute-start.6
  109.3 1.3 collective-permute-start.5
  110.6 23.0 %collective-permute-done.4 = bf16[2,256,256]{1,2,0:T(8,128)(2,1)S(1)} collective-permute-done((bf16[2,256,256]{1,2,0:T(8,128)(2,1)S(1)}, bf16[2,256,256]{1,2,0:T(8,128)(2,1)S(1)}, u32[]{:S(2)}, u32[]{:S(2)}) %collective-permute-start.4) | collective-permute-done | bytes 262176 | tf_op jit(solution)/shard_map/ppermute | solution.py:16
  133.6 6.1 %collective-permute-done.5 = bf16[2,256,256]{1,2,0:T(8,128)(2,1)S(1)} collective-permute-done((bf16[2,256,256]{1,2,0:T(8,128)(2,1)S(1)}, bf16[2,256,256]{1,2,0:T(8,128)(2,1)S(1)}, u32[]{:S(2)}, u32[]{:S(2)}) %collective-permute-start.5) | collective-permute-done | bytes 262176 | tf_op jit(solution)/shard_map/ppermute | solution.py:16
  139.9 1.0 copy.188
  140.9 2.5 %fusion.44 = bf16[256,4,128]{0,2,1:T(8,128)(2,1)S(1)} fusion(bf16[4,256,1280]{1,2,0:T(8,128)(2,1)} %copy-done.2, bf16[2,1280,256]{2,1,0:T(8,128)(2,1)} %copy-done.5), kind=kOutput, calls=%fused_computation.83 | convolution fusion | flops 335806464 | bytes 3211264 | tf_op jit(solution)/shard_map/gre,ed->rgd/dot_general | solution.py:35
  143.5 3.1 %fusion.42 = bf16[256,4,128]{0,2,1:T(8,128)(2,1)} fusion(bf16[4,256,1280]{1,2,0:T(8,128)(2,1)} %copy-done.3, bf16[2,1280,256]{2,1,0:T(8,128)(2,1)} %copy-done.5), kind=kOutput, calls=%fused_computation.81 | convolution fusion | flops 335806464 | bytes 3211264 | tf_op jit(solution)/shard_map/gre,ed->rgd/dot_general | solution.py:35
  146.6 2.2 %fusion.43 = bf16[256,4,128]{0,2,1:T(8,128)(2,1)} fusion(bf16[4,256,1280]{1,2,0:T(8,128)(2,1)S(1)} %copy-done.1, bf16[2,1280,256]{2,1,0:T(8,128)(2,1)} %copy-done.5), kind=kOutput, calls=%fused_computation.82 | convolution fusion | flops 335806464 | bytes 3211264 | tf_op jit(solution)/shard_map/gre,ed->rgd/dot_general | solution.py:35
  148.8 43.8 %all-gather.3.cloned.1.call-done = f32[8,256,256]{2,1,0:T(8,128)} async-done(((f32[2,256,256]{2,1,0:T(8,128)}), f32[8,256,256]{2,1,0:T(8,128)}) %all-gather.3.cloned.1.call-update) | async-done | bytes 2097168 | tf_op jit(solution)/shard_map/all_gather | solution.py:97
  192.7 1.8 reduce_sum.89
  194.5 1.2 copy.190
  195.7 4.3 %all-to-all-start.1 = ((f32[2,256,256]{2,0,1:T(2,128)}), f32[2,256,256]{2,0,1:T(2,128)S(1)}, u32[]{:S(2)}, u32[]{:S(2)}) async-start(f32[2,256,256]{2,0,1:T(2,128)} %copy.190), calls=%async_computation.1 | async-start | bytes 1048576 | tf_op jit(solution)/shard_map/all_to_all | solution.py:98
  199.9 1.6 fusion.41
  201.7 1.4 copy.193
  203.1 4.7 %all-to-all-done.1 = f32[2,256,256]{2,0,1:T(2,128)S(1)} async-done(((f32[2,256,256]{2,0,1:T(2,128)}), f32[2,256,256]{2,0,1:T(2,128)S(1)}, u32[]{:S(2)}, u32[]{:S(2)}) %all-to-all-start.1) | async-done | bytes 524320 | tf_op jit(solution)/shard_map/all_to_all | solution.py:98
  207.8 0.8 copy.248
  (68 shorter events, 4.4 us)
Async XLA Ops:
  7.2 20.5 %copy-start.12 = (bf16[1,256,2048]{2,1,0:T(8,128)(2,1)S(1)}, bf16[1,256,2048]{2,1,0:T(8,128)(2,1)}, u32[]{:S(2)}) copy-start(bf16[1,256,2048]{2,1,0:T(8,128)(2,1)} %param.4) | copy-start | bytes 3145732
  9.6 11.6 %all-to-all-start = ((bf16[4,2,16384]{2,1,0:T(2,128)(2,1)}), bf16[4,2,16384]{2,1,0:T(2,128)(2,1)S(1)}, u32[]{:S(2)}, u32[]{:S(2)}) async-start(bf16[4,2,16384]{2,1,0:T(2,128)(2,1)} %reshape.106), calls=%async_computation | async-start | bytes 524288 | tf_op jit(solution)/shard_map/all_to_all | solution.py:47
  16.2 176.5 %all-gather.3.cloned.1.call-start = ((), (), s32[]{:S(2)}) async-start(), calls=%async_computation.2 | async-start | bytes 2621440 | tf_op jit(solution)/shard_map/all_gather | solution.py:97
  22.6 24.3 %collective-permute-start = (bf16[2,256,256]{2,1,0:T(8,128)(2,1)}, bf16[2,256,256]{2,1,0:T(8,128)(2,1)}, u32[]{:S(2)}, u32[]{:S(2)}) collective-permute-start(bf16[2,256,256]{2,1,0:T(8,128)(2,1)} %bitcast.2), channel_id=1, source_target_pairs={{0,16},{4,20},{8,24},{12,28},{16,32},{20,36},{24,40},{28,44},{32,4... | collective-permute-start | bytes 786440 | tf_op jit(solution)/shard_map/ppermute | solution.py:16
  28.2 71.2 %copy-start.4 = (bf16[1,256,2048]{1,2,0:T(8,128)(2,1)}, bf16[1,256,2048]{1,2,0:T(8,128)(2,1)S(1)}, u32[]{:S(2)}) copy-start(bf16[1,256,2048]{1,2,0:T(8,128)(2,1)S(1)} %copy.144) | copy-start | bytes 3145732
  28.2 20.7 %collective-permute-start.2 = (bf16[2,256,256]{2,1,0:T(8,128)(2,1)}, bf16[2,256,256]{2,1,0:T(8,128)(2,1)}, u32[]{:S(2)}, u32[]{:S(2)}) collective-permute-start(bf16[2,256,256]{2,1,0:T(8,128)(2,1)} %bitcast.2), channel_id=1, source_target_pairs={{0,8},{4,12},{8,16},{12,20},{16,24},{20,28},{24,32},{28,36},{32,40... | collective-permute-start | bytes 786440 | tf_op jit(solution)/shard_map/ppermute | solution.py:16
  32.4 15.5 %collective-permute-start.1 = (bf16[2,256,256]{2,1,0:T(8,128)(2,1)}, bf16[2,256,256]{2,1,0:T(8,128)(2,1)}, u32[]{:S(2)}, u32[]{:S(2)}) collective-permute-start(bf16[2,256,256]{2,1,0:T(8,128)(2,1)} %bitcast.2), channel_id=1, source_target_pairs={{0,12},{4,16},{8,20},{12,24},{16,28},{20,32},{24,36},{28,40},{32,4... | collective-permute-start | bytes 786440 | tf_op jit(solution)/shard_map/ppermute | solution.py:16
  40.7 46.5 %copy-start.6 = (bf16[1,256,2048]{1,2,0:T(8,128)(2,1)}, bf16[1,256,2048]{1,2,0:T(8,128)(2,1)S(1)}, u32[]{:S(2)}) copy-start(bf16[1,256,2048]{1,2,0:T(8,128)(2,1)S(1)} %copy.142) | copy-start | bytes 3145732
  44.3 6.6 %collective-permute-start.3 = (bf16[2,256,256]{2,1,0:T(8,128)(2,1)}, bf16[2,256,256]{2,1,0:T(8,128)(2,1)S(1)}, u32[]{:S(2)}, u32[]{:S(2)}) collective-permute-start(bf16[2,256,256]{2,1,0:T(8,128)(2,1)} %bitcast.2), channel_id=1, source_target_pairs={{0,4},{4,8},{8,12},{12,16},{16,20},{20,24},{24,28},{28,32},{32,36}... | collective-permute-start | bytes 786440 | tf_op jit(solution)/shard_map/ppermute | solution.py:16
  51.9 46.2 %copy-start.5 = (bf16[2,1280,256]{2,1,0:T(8,128)(2,1)}, bf16[2,1280,256]{2,1,0:T(8,128)(2,1)S(1)}, u32[]{:S(2)}) copy-start(bf16[2,1280,256]{2,1,0:T(8,128)(2,1)S(1)} %constant_dynamic-update-slice_fusion) | copy-start | bytes 3932164
  72.5 6.3 %slice-start.6 = ((s8[5242880]{0:T(1024)(128)(4,1)}), s8[4194304]{0:T(1024)(128)(4,1)S(1)}, s32[]{:S(2)}) async-start(s8[5242880]{0:T(1024)(128)(4,1)} %bitcast.226), calls=%async_computation.9 | async-start | bytes 8388608
  76.5 1.0 copy-start.11
  76.5 2.3 %slice-start.7 = ((s8[5242880]{0:T(1024)(128)(4,1)}), s8[1048576]{0:T(1024)(128)(4,1)S(1)}, s32[]{:S(2)}) async-start(s8[5242880]{0:T(1024)(128)(4,1)} %bitcast.226), calls=%async_computation.10 | async-start | bytes 2097152
  78.8 2.7 %slice-start.4 = ((s8[5242880]{0:T(1024)(128)(4,1)}), s8[4194304]{0:T(1024)(128)(4,1)S(1)}, s32[]{:S(2)}) async-start(s8[5242880]{0:T(1024)(128)(4,1)} %bitcast.224), calls=%async_computation.7 | async-start | bytes 8388608
  78.8 3.4 %slice-start.5 = ((s8[5242880]{0:T(1024)(128)(4,1)}), s8[1048576]{0:T(1024)(128)(4,1)S(1)}, s32[]{:S(2)}) async-start(s8[5242880]{0:T(1024)(128)(4,1)} %bitcast.224), calls=%async_computation.8 | async-start | bytes 2097152
  79.9 1.5 copy-start.2
  83.8 1.0 copy-start.10
  86.1 2.7 %slice-start.2 = ((s8[5242880]{0:T(1024)(128)(4,1)}), s8[4194304]{0:T(1024)(128)(4,1)S(1)}, s32[]{:S(2)}) async-start(s8[5242880]{0:T(1024)(128)(4,1)} %bitcast.222), calls=%async_computation.5 | async-start | bytes 8388608
  86.1 3.4 %slice-start.3 = ((s8[5242880]{0:T(1024)(128)(4,1)}), s8[1048576]{0:T(1024)(128)(4,1)S(1)}, s32[]{:S(2)}) async-start(s8[5242880]{0:T(1024)(128)(4,1)} %bitcast.222), calls=%async_computation.6 | async-start | bytes 2097152
  87.2 1.6 copy-start.3
  89.5 1.4 copy-start.9
  93.2 2.4 %slice-start = ((s8[5242880]{0:T(1024)(128)(4,1)}), s8[4194304]{0:T(1024)(128)(4,1)S(1)}, s32[]{:S(2)}) async-start(s8[5242880]{0:T(1024)(128)(4,1)} %bitcast.220), calls=%async_computation.3 | async-start | bytes 8388608
  93.2 3.4 %slice-start.1 = ((s8[5242880]{0:T(1024)(128)(4,1)}), s8[1048576]{0:T(1024)(128)(4,1)S(1)}, s32[]{:S(2)}) async-start(s8[5242880]{0:T(1024)(128)(4,1)} %bitcast.220), calls=%async_computation.4 | async-start | bytes 2097152
  94.4 8.5 %copy-start = (bf16[4,256,1280]{1,2,0:T(8,128)(2,1)}, bf16[4,256,1280]{1,2,0:T(8,128)(2,1)S(1)}, u32[]{:S(2)}) copy-start(bf16[4,256,1280]{1,2,0:T(8,128)(2,1)S(1)} %fusion.13) | copy-start | bytes 7864324
  96.7 1.4 copy-start.8
  100.4 2.6 %copy-start.7 = (bf16[1,256,2048]{1,2,0:T(8,128)(2,1)S(1)}, bf16[1,256,2048]{1,2,0:T(8,128)(2,1)}, u32[]{:S(2)}) copy-start(bf16[1,256,2048]{1,2,0:T(8,128)(2,1)} %copy-done.6) | copy-start | bytes 3145732
  105.4 28.2 %collective-permute-start.4 = (bf16[2,256,256]{1,2,0:T(8,128)(2,1)S(1)}, bf16[2,256,256]{1,2,0:T(8,128)(2,1)S(1)}, u32[]{:S(2)}, u32[]{:S(2)}) collective-permute-start(bf16[2,256,256]{1,2,0:T(8,128)(2,1)S(1)} %get-tuple-element.10), channel_id=1, source_target_pairs={{16,0},{20,4},{24,8},{28,12},{32,16},{36,20},{40,24},{44,28},{48,3... | collective-permute-start | bytes 786440 | tf_op jit(solution)/shard_map/ppermute | solution.py:16
  106.7 26.9 %collective-permute-start.7 = (bf16[2,256,256]{1,2,0:T(8,128)(2,1)S(1)}, bf16[2,256,256]{1,2,0:T(8,128)(2,1)S(1)}, u32[]{:S(2)}, u32[]{:S(2)}) collective-permute-start(bf16[2,256,256]{1,2,0:T(8,128)(2,1)S(1)} %get-tuple-element.11), channel_id=1, source_target_pairs={{4,0},{8,4},{12,8},{16,12},{20,16},{24,20},{28,24},{32,28},{36,32}... | collective-permute-start | bytes 786440 | tf_op jit(solution)/shard_map/ppermute | solution.py:16
  108.0 25.6 %collective-permute-start.6 = (bf16[2,256,256]{1,2,0:T(8,128)(2,1)S(1)}, bf16[2,256,256]{1,2,0:T(8,128)(2,1)S(1)}, u32[]{:S(2)}, u32[]{:S(2)}) collective-permute-start(bf16[2,256,256]{1,2,0:T(8,128)(2,1)S(1)} %get-tuple-element.12), channel_id=1, source_target_pairs={{8,0},{12,4},{16,8},{20,12},{24,16},{28,20},{32,24},{36,28},{40,32... | collective-permute-start | bytes 786440 | tf_op jit(solution)/shard_map/ppermute | solution.py:16
  109.3 30.4 %collective-permute-start.5 = (bf16[2,256,256]{1,2,0:T(8,128)(2,1)S(1)}, bf16[2,256,256]{1,2,0:T(8,128)(2,1)S(1)}, u32[]{:S(2)}, u32[]{:S(2)}) collective-permute-start(bf16[2,256,256]{1,2,0:T(8,128)(2,1)S(1)} %get-tuple-element.13), channel_id=1, source_target_pairs={{12,0},{16,4},{20,8},{24,12},{28,16},{32,20},{36,24},{40,28},{44,3... | collective-permute-start | bytes 786440 | tf_op jit(solution)/shard_map/ppermute | solution.py:16
  140.9 5.7 %copy-start.1 = (bf16[4,256,1280]{1,2,0:T(8,128)(2,1)S(1)}, bf16[4,256,1280]{1,2,0:T(8,128)(2,1)}, u32[]{:S(2)}) copy-start(bf16[4,256,1280]{1,2,0:T(8,128)(2,1)} %copy-done) | copy-start | bytes 7864324
  195.7 12.1 %all-to-all-start.1 = ((f32[2,256,256]{2,0,1:T(2,128)}), f32[2,256,256]{2,0,1:T(2,128)S(1)}, u32[]{:S(2)}, u32[]{:S(2)}) async-start(f32[2,256,256]{2,0,1:T(2,128)} %copy.190), calls=%async_computation.1 | async-start | bytes 1048576 | tf_op jit(solution)/shard_map/all_to_all | solution.py:98
  199.9 1.6 copy-start.13
  199.9 1.6 copy-start.14
Sparse Core Ops, SparseCore 0:
  141.1 51.5 all-gather.2
